TPU v7x, 256 devices: a whole 4x4x8 slice. The times are simulated.
256 devices in a mesh: grp: 8 (over x, core), dev: 32 (over z, y).
Axes of the slice: x: 4, y: 4, z: 8, core: 2. Of those that a mesh axis runs over, the one named last changes fastest.
Arguments:
- references: bfloat16 [192, 2048], P('dev'), may hold values from -4 to 4
- particles: bfloat16 [2048, 65536], P(None, ('grp', 'dev')), may hold values from -1300 to 1300
- defocus_bin: int32 [65536], P(('grp', 'dev')), may hold values from 0 to 63
- contrast_table: float32 [64, 32], replicated, may hold values from 0.1 to 1
- noise_power: float32 [32], replicated, may hold values from 300 to 3000
- class_prior: float32 [192], replicated, may hold values from -3 to 3
Outputs:
- new_references: float32 [192, 2048], P('dev')
- occupancy: float32 [192], P('dev')
All inputs are finite; a program needn't handle non-finite values.
Results may differ from a plain program's by a relative error of at most 0.0015.
Values may be sent and summed in bfloat16 or wider, within the bound.
No kernel may reach another device: no remote copies, remote signals or barrier semaphores. Data moves between devices by JAX's collectives and lax.ppermute only.
A program may use at most 64 MiB of HBM per device.

v0:
```python
import math
import jax
import jax.numpy as jnp
from jax import lax
from jax.sharding import PartitionSpec as P

Q = 32
M = 32
R = 128
CLS_DEV = 6


def angle_tables(cycle_freqs, count_turns):
    freq_index = jnp.arange(cycle_freqs, dtype=jnp.int32)
    turn_index = jnp.arange(count_turns, dtype=jnp.int32)
    wrapped = freq_index[:, None] * turn_index[None, :] % count_turns
    phases = 2.0 * math.pi / count_turns * wrapped.astype(jnp.float32)
    factor = jnp.where(freq_index == 0, 1.0, 2.0).astype(jnp.float32)[:, None]
    cosine = jnp.cos(phases)
    sine_part = jnp.sin(phases)
    score_table = jnp.stack([factor * cosine, factor * sine_part], 0).astype(jnp.bfloat16)
    turn_table = jnp.stack([cosine, sine_part], 0).astype(jnp.bfloat16)
    return (score_table, turn_table)


def particle_terms(particles, defocus_bin, contrast_table, noise_power):
    columns = particles.shape[1]
    cycle_count = contrast_table.shape[1]
    freq_count = particles.shape[0] // (2 * cycle_count)
    onehot = (
        defocus_bin[None, :] == jnp.arange(contrast_table.shape[0], dtype=jnp.int32)[:, None]
    ).astype(jnp.float32)
    contrast = jnp.dot(contrast_table.T, onehot, precision=lax.Precision.HIGHEST)
    scaled = contrast / noise_power[:, None]
    power_term = contrast * scaled
    weighted = (
        particles.astype(jnp.float32).reshape(freq_count, 2, cycle_count, columns)
        * scaled[None, None]
    ).astype(jnp.bfloat16)
    return (weighted.reshape(freq_count, 2 * cycle_count, columns), power_term)


def class_rows(class_block):
    classes = class_block.shape[0]
    class_grid = class_block.reshape(classes, M, 2, Q)
    real_part = class_grid[:, :, 0, :]
    imag_part = class_grid[:, :, 1, :]
    rows_real = jnp.concatenate([real_part, imag_part], -1)
    rows_imag = jnp.concatenate([-imag_part, real_part], -1)
    stacked = jnp.stack([rows_real, rows_imag], 0)
    factor = jnp.where(jnp.arange(M) == 0, 1.0, 2.0).astype(jnp.float32)
    squares = class_grid.astype(jnp.float32) ** 2
    cycle_power = jnp.sum(jnp.sum(squares, axis=2) * factor[None, :, None], axis=1)
    return (stacked, cycle_power)


def block_rows(total_rows):
    return CLS_DEV * math.gcd(total_rows // CLS_DEV, 4)


def local(references, particles, defocus_bin, contrast_table, noise_power, class_prior):
    weighted, power_term = particle_terms(particles, defocus_bin, contrast_table, noise_power)
    score_table, turn_table = angle_tables(M, R)
    columns = particles.shape[1]
    classes_total = CLS_DEV * lax.axis_size("dev")

    def block_scores(class_block, first_row):
        stacked, cycle_power = class_rows(class_block)
        prior_part = lax.dynamic_slice_in_dim(class_prior, first_row, class_block.shape[0], 0)
        crossed = jnp.einsum(
            "pkmc,mcb->pmkb", stacked, weighted, preferred_element_type=jnp.float32
        ).astype(jnp.bfloat16)
        scores = jnp.einsum(
            "pmkb,pmr->krb", crossed, score_table, preferred_element_type=jnp.float32
        )
        penalty = jnp.dot(cycle_power, power_term, precision=lax.Precision.HIGHEST)
        return scores - 0.5 * penalty[:, None, :] + prior_part[:, None, None]

    initial = (jnp.full((columns,), -1e30, jnp.float32), jnp.zeros((columns,), jnp.float32))
    empty_sums = (
        jnp.zeros((classes_total, 2 * M * Q), jnp.float32),
        jnp.zeros((classes_total, Q), jnp.float32),
        jnp.zeros((classes_total,), jnp.float32),
    )
    gathered = lax.all_gather(references, "dev", axis=0, tiled=True)
    height = block_rows(gathered.shape[0])
    block_count = gathered.shape[0] // height
    blocks = gathered.reshape(block_count, height, gathered.shape[1])

    def one_block(current, block_item):
        class_block, offset = block_item
        scores = block_scores(class_block, offset * height)
        block_max = jnp.max(scores, axis=(0, 1))
        new_max = jnp.maximum(current[0], block_max)
        block_total = jnp.sum(jnp.exp(scores - new_max[None, None, :]), axis=(0, 1))
        return ((new_max, current[1] * jnp.exp(current[0] - new_max) + block_total), None)

    result, unused = lax.scan(
        one_block, initial, (blocks, jnp.arange(block_count, dtype=jnp.int32))
    )
    log_norm = result[0] + jnp.log(result[1])
    add_height = block_rows(gathered.shape[0])
    block_count = gathered.shape[0] // add_height
    blocks = gathered.reshape(block_count, add_height, gathered.shape[1])

    def one_block(current, block_item):
        class_block, offset = block_item
        row_start = offset * add_height
        scores = block_scores(class_block, row_start)
        responsibility = jnp.exp(scores - log_norm[None, None, :]).astype(jnp.bfloat16)
        spectra = jnp.einsum(
            "krb,pmr->pmkb", responsibility, turn_table, preferred_element_type=jnp.float32
        ).astype(jnp.bfloat16)
        products = jnp.einsum(
            "pmkb,mcb->kpmc", spectra, weighted, preferred_element_type=jnp.float32
        )
        real_sum = products[:, 0, :, :Q] + products[:, 1, :, Q:]
        imag_sum = products[:, 0, :, Q:] - products[:, 1, :, :Q]
        numerator = jnp.stack([real_sum, imag_sum], 2).reshape(add_height, 2 * M * Q)
        class_weight = jnp.sum(responsibility.astype(jnp.float32), axis=1)
        cycle_sum = jnp.dot(class_weight, power_term.T, precision=lax.Precision.HIGHEST)
        class_mass = jnp.sum(class_weight, axis=1)
        updated = (
            lax.dynamic_update_slice_in_dim(current[0], numerator, row_start, 0),
            lax.dynamic_update_slice_in_dim(current[1], cycle_sum, row_start, 0),
            lax.dynamic_update_slice_in_dim(current[2], class_mass, row_start, 0),
        )
        return (updated, None)

    result, unused = lax.scan(
        one_block, empty_sums, (blocks, jnp.arange(block_count, dtype=jnp.int32))
    )
    numer_all, cycles_all, mass_all = result
    merged = lax.psum((numer_all, cycles_all, mass_all), ("grp", "dev"))
    own_start = lax.axis_index("dev") * CLS_DEV
    numerator = lax.dynamic_slice_in_dim(merged[0], own_start, CLS_DEV, 0)
    cycle_sum = lax.dynamic_slice_in_dim(merged[1], own_start, CLS_DEV, 0)
    class_mass = lax.dynamic_slice_in_dim(merged[2], own_start, CLS_DEV, 0)
    new_references = (numerator.reshape(CLS_DEV, M, 2, Q) / cycle_sum[:, None, None, :]).reshape(
        CLS_DEV, 2 * M * Q
    )
    particle_total = columns * lax.axis_size("grp") * lax.axis_size("dev")
    occupancy = class_mass * (classes_total / particle_total)
    return (new_references, occupancy)


def solution(mesh):
    return jax.shard_map(
        local,
        mesh=mesh,
        in_specs=(P("dev", None), P(None, ("grp", "dev")), P(("grp", "dev")), P(), P(), P()),
        out_specs=(P("dev", None), P("dev")),
        check_vma=False,
    )
```

profile of v0, /device:TPU:2, one launch (start us, length us, event | category | flops | bytes accessed | tf_op | source)
XLA Modules:
  0.0 525.7 jit_solution(9444845568496355798)
XLA Ops:
  7.5 53.8 %all-gather = bf16[32,6,2048]{2,1,0:T(8,128)(2,1)S(1)} all-gather(bf16[1,6,2048]{2,1,0:T(8,128)(2,1)} %bitcast.179), channel_id=1, replica_groups=mesh['grp'=8,'dev'=32] {'dev'}, dimensions={0}, use_global_device_ids=true | all-gather | bytes 811008 | tf_op jit(solution)/shard_map/all_gather | solution.py:85
  64.5 87.8 %while.28 = (s32[]{:T(128)}, f32[256]{0:T(256)S(1)}, f32[256]{0:T(256)S(1)}, bf16[8,24,2048]{2,1,0:T(8,128)(2,1)}, bf16[32,64,256]{2,1,0:T(8,128)(2,1)}, /*index...) while((s32[]{:T(128)}, f32[256]{0:T(256)S(1)}, ...), condition=%wide.region_5.6_spmd.clone, body=%wide.region_0.5_spmd.clone.sunk | while | flops 159947328 | bytes 10727242 | solution.py:98
  67.3 2.5 fusion.111
  72.5 2.0 fusion.112
  78.3 2.5 fusion.111
  83.5 2.0 fusion.112
  89.2 2.5 fusion.111
  94.5 2.0 fusion.112
  100.2 2.5 fusion.111
  105.5 2.0 fusion.112
  111.2 2.5 fusion.111
  116.5 2.0 fusion.112
  122.2 2.5 fusion.111
  127.4 2.0 fusion.112
  133.2 2.5 fusion.111
  138.4 2.0 fusion.112
  144.2 2.5 fusion.111
  149.4 2.0 fusion.112
  152.6 106.6 %while.27 = (s32[]{:T(128)}, f32[192,2048]{1,0:T(8,128)S(1)}, f32[192,32]{1,0:T(8,128)S(1)}, f32[192]{0:T(256)S(1)}, bf16[8,24,2048]{2,1,0:T(8,128)(2,1)}, /*ind...) while((s32[]{:T(128)}, f32[192,2048]{1,0:T(8,128)S(1)}, ...), condition=%wide.region_11.12_spmd, body=%wide.region_6.11_spmd.sunk | while | flops 313785664 | bytes 12832803 | solution.py:130
  161.6 2.0 convolution_bitcast_fusion.3
  168.9 1.6 fusion.101
  174.9 2.0 convolution_bitcast_fusion.3
  188.2 2.0 convolution_bitcast_fusion.3
  195.5 1.6 fusion.101
  201.5 2.0 convolution_bitcast_fusion.3
  214.9 2.0 convolution_bitcast_fusion.3
  222.1 1.6 fusion.101
  228.2 2.0 convolution_bitcast_fusion.3
  241.5 2.0 convolution_bitcast_fusion.3
  254.8 2.0 convolution_bitcast_fusion.3
  260.4 73.8 %all-reduce = (f32[192,32]{1,0:T(8,128)S(1)}, f32[192]{0:T(256)S(1)}) all-reduce(f32[192,32]{1,0:T(8,128)S(1)} %get-tuple-element.117, f32[192]{0:T(256)S(1)} %get-tuple-element.118), channel_id=1, replica_groups=mesh['grp'=8,'dev'=32] {'grp','dev'}, use_global_device_ids=true, to_apply=%region_13.14 | all-reduce | flops 6336 | bytes 50688 | tf_op jit(solution)/shard_map/psum | solution.py:134
  335.1 182.2 %all-reduce.3.cloned.1.call-done = f32[192,2048]{1,0:T(8,128)} async-done(((f32[192,2048]{1,0:T(8,128)}), f32[192,2048]{1,0:T(8,128)}) %all-reduce.3.cloned.1.call-update) | async-done | bytes 1572880 | tf_op jit(solution)/shard_map/psum | solution.py:134
  (341 shorter events, 133.2 us)
Async XLA Ops:
  7.2 55.2 %copy-start = (f32[64,32]{0,1:T(8,128)S(1)}, f32[64,32]{0,1:T(8,128)}, u32[]{:S(2)}) copy-start(f32[64,32]{0,1:T(8,128)} %param.13) | copy-start | bytes 24580
  7.2 56.1 %copy-start.2 = (bf16[2048,256]{1,0:T(8,128)(2,1)S(1)}, bf16[2048,256]{1,0:T(8,128)(2,1)}, u32[]{:S(2)}) copy-start(bf16[2048,256]{1,0:T(8,128)(2,1)} %param.11) | copy-start | bytes 3145732
  7.2 57.3 %copy-start.3 = (f32[192]{0:T(256)S(1)}, f32[192]{0:T(256)}, u32[]{:S(2)}) copy-start(f32[192]{0:T(256)} %param.15) | copy-start | bytes 2308
  7.2 510.1 %all-reduce.3.cloned.1.call-start = ((), (), s32[]{:S(2)}) async-start(), calls=%async_computation | async-start | bytes 3145728 | tf_op jit(solution)/shard_map/psum | solution.py:134
  259.2 1.1 copy-start.1
Sparse Core Ops, SparseCore 0:
  260.5 256.7 all-reduce.2
where the time goes:
time: 528 us; the launch traced here: 526 us
  waiting for transfers between devices  182 us (34%)
  blocking collectives  128 us (24%)
  matrix products  82.1 us (16%)
  local copies, waits for them, and re-layouts  64.7 us (12%)
  other arithmetic  42.8 us (8%)
  between operations  14.2 us (3%)
  loops' own time  12.1 us (2%)
    psum x1, waiting for transfers between devices, local(): merged = lax.psum((numer_all, cycles_all, mass_all), ('grp', 'dev'))  182 us
    psum x1, blocking collectives, local(): merged = lax.psum((numer_all, cycles_all, mass_all), ('grp', 'dev'))  73.8 us
    all_gather x1, blocking collectives, local(): gathered = lax.all_gather(references, 'dev', axis=0, tiled=True)  53.8 us
    dot_general x16, matrix products, block_scores(): jnp.einsum('pkmc,mcb->pmkb', stacked, weighted, preferred_element_type=jn...  32.7 us
    dot_general x16, matrix products, block_scores(): jnp.einsum('pmkb,pmr->krb', crossed, score_table, preferred_element_type=...  26.3 us
    dynamic_slice x32, local copies, waits for them, and re-layouts, local(): lax.scan(one_block, initial, (blocks, jnp.arange(block_count, dtype=jnp.i...  23.9 us
    reduce_sum x16, other arithmetic, class_rows(): jnp.sum(squares, axis=2) * factor[None, :, None]  18.6 us
    dot_general x8, matrix products, one_block(): jnp.einsum('pmkb,mcb->kpmc', spectra, weighted, preferred_element_type=jn...  15.7 us
  transfers between devices with their start and end apart: 1, of which 1 were waited for; matrix products, arithmetic and copies ran while one was open for 0% of the time, Pallas kernels for 0%

commit v1 on v0

--- a/solution.py
+++ b/solution.py
@@ -1,13 +1,25 @@
+import functools
 import math
 import jax
 import jax.numpy as jnp
 from jax import lax
 from jax.sharding import PartitionSpec as P
+from jax.lax import all_to_all, psum
 
 Q = 32
 M = 32
 R = 128
 CLS_DEV = 6
+
+
+def _balance_cube(block_in, named_axis):
+    local_part = jnp.concatenate(
+        all_to_all(jnp.stack([block_in] * psum(1, named_axis)), named_axis, 0, 0), axis=0
+    )
+    return local_part
+
+
+end_pipes_for = functools.partial(_balance_cube, named_axis="dev")
 
 
 def angle_tables(cycle_freqs, count_turns):
@@ -82,7 +94,7 @@
         jnp.zeros((classes_total, Q), jnp.float32),
         jnp.zeros((classes_total,), jnp.float32),
     )
-    gathered = lax.all_gather(references, "dev", axis=0, tiled=True)
+    gathered = end_pipes_for(references)
     height = block_rows(gathered.shape[0])
     block_count = gathered.shape[0] // height
     blocks = gathered.reshape(block_count, height, gathered.shape[1])

time: 528 us -> 513 us (0.972)
  blocking collectives: 128 us -> 74.5 us
  waiting for transfers between devices: 182 us -> 208 us
  starting transfers between devices: 0.04 us -> 11.7 us
    all_gather x1 -> x0, blocking collectives: 53.8 us -> none  [local(): gathered = lax.all_gather(references, 'dev', axis=0, tiled=True)]
    all_to_all x0 -> x1, waiting for transfers between devices: none -> 26.3 us  [_balance_cube(): all_to_all(jnp.stack([block_in] * psum(1, named_axis)), named_axis, 0, 0)]
    all_to_all x0 -> x1, starting transfers between devices: none -> 11.6 us  [_balance_cube(): all_to_all(jnp.stack([block_in] * psum(1, named_axis)), named_axis, 0, 0)]
  transfers between devices with their start and end apart: 1 -> 2, of which waited for: 1 -> 2; matrix products, arithmetic and copies ran while one was open for 0% -> 0% of each run, Pallas kernels for 0% -> 0%
where the time goes in v1:
time: 513 us; the launch traced here: 511 us
  waiting for transfers between devices  208 us (41%)
  matrix products  81.5 us (16%)
  blocking collectives  74.5 us (15%)
  local copies, waits for them, and re-layouts  66.7 us (13%)
  other arithmetic  42.8 us (8%)
  between operations  14.2 us (3%)
  loops' own time  12.1 us (2%)
  starting transfers between devices  11.7 us (2%)
    psum x1, waiting for transfers between devices, local(): merged = lax.psum((numer_all, cycles_all, mass_all), ('grp', 'dev'))  181 us
    psum x1, blocking collectives, local(): merged = lax.psum((numer_all, cycles_all, mass_all), ('grp', 'dev'))  74.5 us
    dot_general x16, matrix products, block_scores(): jnp.einsum('pkmc,mcb->pmkb', stacked, weighted, preferred_element_type=jn...  32.7 us
    all_to_all x1, waiting for transfers between devices, _balance_cube(): all_to_all(jnp.stack([block_in] * psum(1, named_axis)), named_axis, 0, 0)  26.3 us
    dot_general x16, matrix products, block_scores(): jnp.einsum('pmkb,pmr->krb', crossed, score_table, preferred_element_type=...  26.3 us
    dynamic_slice x32, local copies, waits for them, and re-layouts, local(): lax.scan(one_block, initial, (blocks, jnp.arange(block_count, dtype=jnp.i...  23.9 us
    reduce_sum x16, other arithmetic, class_rows(): jnp.sum(squares, axis=2) * factor[None, :, None]  18.6 us
    dot_general x8, matrix products, one_block(): jnp.einsum('pmkb,mcb->kpmc', spectra, weighted, preferred_element_type=jn...  15.7 us
  transfers between devices with their start and end apart: 2, of which 2 were waited for; matrix products, arithmetic and copies ran while one was open for 0% of the time, Pallas kernels for 0%

profile of v1, /device:TPU:2, one launch (start us, length us, event | category | flops | bytes accessed | tf_op | source)
XLA Modules:
  0.0 510.9 jit_solution(3489984348825701169)
XLA Ops:
  7.2 2.0 stack.22
  9.2 11.6 %all-to-all-start = ((bf16[32,6,2048]{2,1,0:T(8,128)(2,1)}), bf16[32,6,2048]{2,1,0:T(8,128)(2,1)S(1)}, u32[]{:S(2)}, u32[]{:S(2)}) async-start(bf16[32,6,2048]{2,1,0:T(8,128)(2,1)} %stack.22), calls=%async_computation | async-start | bytes 2097152 | tf_op jit(solution)/shard_map/all_to_all | solution.py:17
  22.6 26.3 %all-to-all-done = bf16[32,6,2048]{2,1,0:T(8,128)(2,1)S(1)} async-done(((bf16[32,6,2048]{2,1,0:T(8,128)(2,1)}), bf16[32,6,2048]{2,1,0:T(8,128)(2,1)S(1)}, u32[]{:S(2)}, u32[]{:S(2)}) %all-to-all-start) | async-done | bytes 786464 | tf_op jit(solution)/shard_map/all_to_all | solution.py:17
  50.1 87.8 %while.28 = (s32[]{:T(128)}, f32[256]{0:T(256)S(1)}, f32[256]{0:T(256)S(1)}, bf16[8,24,2048]{2,1,0:T(8,128)(2,1)}, bf16[32,64,256]{2,1,0:T(8,128)(2,1)}, /*index...) while((s32[]{:T(128)}, f32[256]{0:T(256)S(1)}, ...), condition=%wide.region_5.6_spmd.clone, body=%wide.region_0.5_spmd.clone.sunk | while | flops 159947328 | bytes 10727242 | solution.py:110
  52.9 2.5 fusion.111
  58.1 2.0 fusion.112
  63.9 2.5 fusion.111
  69.1 2.0 fusion.112
  74.8 2.5 fusion.111
  80.1 2.0 fusion.112
  85.8 2.5 fusion.111
  91.1 2.0 fusion.112
  96.8 2.5 fusion.111
  102.1 2.0 fusion.112
  107.8 2.5 fusion.111
  113.0 2.0 fusion.112
  118.8 2.5 fusion.111
  124.0 2.0 fusion.112
  129.8 2.5 fusion.111
  135.0 2.0 fusion.112
  138.2 106.6 %while.27 = (s32[]{:T(128)}, f32[192,2048]{1,0:T(8,128)S(1)}, f32[192,32]{1,0:T(8,128)S(1)}, f32[192]{0:T(256)S(1)}, bf16[8,24,2048]{2,1,0:T(8,128)(2,1)}, /*ind...) while((s32[]{:T(128)}, f32[192,2048]{1,0:T(8,128)S(1)}, ...), condition=%wide.region_11.12_spmd, body=%wide.region_6.11_spmd.sunk | while | flops 313785664 | bytes 12832803 | solution.py:142
  147.2 2.0 convolution_bitcast_fusion.3
  160.5 2.0 convolution_bitcast_fusion.3
  173.8 2.0 convolution_bitcast_fusion.3
  187.1 2.0 convolution_bitcast_fusion.3
  194.4 1.6 fusion.101
  200.4 2.0 convolution_bitcast_fusion.3
  213.7 2.0 convolution_bitcast_fusion.3
  227.0 2.0 convolution_bitcast_fusion.3
  240.3 2.0 convolution_bitcast_fusion.3
  246.0 74.5 %all-reduce = (f32[192,32]{1,0:T(8,128)S(1)}, f32[192]{0:T(256)S(1)}) all-reduce(f32[192,32]{1,0:T(8,128)S(1)} %get-tuple-element.117, f32[192]{0:T(256)S(1)} %get-tuple-element.118), channel_id=1, replica_groups=mesh['grp'=8,'dev'=32] {'grp','dev'}, use_global_device_ids=true, to_apply=%region_13.14 | all-reduce | flops 6336 | bytes 50688 | tf_op jit(solution)/shard_map/psum | solution.py:146
  321.3 181.1 %all-reduce.3.cloned.1.call-done = f32[192,2048]{1,0:T(8,128)} async-done(((f32[192,2048]{1,0:T(8,128)}), f32[192,2048]{1,0:T(8,128)}) %all-reduce.3.cloned.1.call-update) | async-done | bytes 1572880 | tf_op jit(solution)/shard_map/psum | solution.py:146
  (347 shorter events, 135.8 us)
Async XLA Ops:
  7.2 14.0 %copy-start = (f32[64,32]{0,1:T(8,128)S(1)}, f32[64,32]{0,1:T(8,128)}, u32[]{:S(2)}) copy-start(f32[64,32]{0,1:T(8,128)} %param.13) | copy-start | bytes 24580
  7.2 14.0 %copy-start.3 = (s32[256]{0:T(256)S(1)}, s32[256]{0:T(256)}, u32[]{:S(2)}) copy-start(s32[256]{0:T(256)} %param.12) | copy-start | bytes 3076
  7.2 14.0 %copy-start.5 = (f32[32]{0:T(128)S(1)}, f32[32]{0:T(128)}, u32[]{:S(2)}) copy-start(f32[32]{0:T(128)} %param.14) | copy-start | bytes 388
  7.2 14.1 %copy-start.2 = (bf16[2048,256]{1,0:T(8,128)(2,1)S(1)}, bf16[2048,256]{1,0:T(8,128)(2,1)}, u32[]{:S(2)}) copy-start(bf16[2048,256]{1,0:T(8,128)(2,1)} %param.11) | copy-start | bytes 3145732
  9.2 40.9 %copy-start.4 = (f32[192]{0:T(256)S(1)}, f32[192]{0:T(256)}, u32[]{:S(2)}) copy-start(f32[192]{0:T(256)} %param.15) | copy-start | bytes 2308
  9.2 39.7 %all-to-all-start = ((bf16[32,6,2048]{2,1,0:T(8,128)(2,1)}), bf16[32,6,2048]{2,1,0:T(8,128)(2,1)S(1)}, u32[]{:S(2)}, u32[]{:S(2)}) async-start(bf16[32,6,2048]{2,1,0:T(8,128)(2,1)} %stack.22), calls=%async_computation | async-start | bytes 2097152 | tf_op jit(solution)/shard_map/all_to_all | solution.py:17
  20.8 481.7 %all-reduce.3.cloned.1.call-start = ((), (), s32[]{:S(2)}) async-start(), calls=%async_computation.1 | async-start | bytes 3145728 | tf_op jit(solution)/shard_map/psum | solution.py:146
  244.8 1.1 copy-start.1
Sparse Core Ops, SparseCore 0:
  246.1 256.3 all-reduce.2
